TPU v7x, 512 devices: a whole 4x8x8 slice. The times are simulated.
512 devices in a mesh: dp: 32 (over x, z_lo, core), ctx: 16 (over z_hi, y).
Axes of the slice: x: 4, y: 8, z: 8 (z_hi: 2, z_lo: 4; z = z_hi * 4 + z_lo), core: 2. Of those that a mesh axis runs over, the one named last changes fastest.
Arguments:
- queries: bfloat16 [32, 16, 128, 2048], P('dp', 'ctx'), may hold values from -2.5 to 2.5
- rotated_key_rows: bfloat16 [32, 16, 128, 512], P('dp', 'ctx'), may hold values from -2.5 to 2.5
- values: bfloat16 [32, 16, 128, 512], P('dp', 'ctx'), may hold values from -6 to 6
- cotangent: bfloat16 [32, 16, 128, 2048], P('dp', 'ctx'), may hold values from -6 to 6
- hidden: bfloat16 [32, 16, 128, 4096], P('dp', 'ctx'), may hold values from -6 to 6
- adapter_down_weight: bfloat16 [4096, 16], replicated, may hold values from -0.09375 to 0.09375
- adapter_up_weight: bfloat16 [16, 512], replicated, may hold values from -1.5 to 1.5
- segment_text_length: int32 [32, 16], P('dp', 'ctx'), may hold values from 19 to 78, as said below
Outputs:
- grad_queries: bfloat16 [32, 16, 128, 2048], P('dp', 'ctx')
- grad_keys: bfloat16 [32, 16, 128, 512], P('dp', 'ctx')
- grad_values: bfloat16 [32, 16, 128, 512], P('dp', 'ctx')
- grad_down: float32 [4096, 16], replicated
- grad_up: float32 [16, 512], replicated
Inputs may be any that keep to these rules, and one draw needn't show every extreme that they name: `segment_text_length`: every log has a segment with exactly 78 text tokens and another with the fewest.
All inputs are finite; a program needn't handle non-finite values.
Results may differ from a plain program's by a relative error of at most 0.0019.
The roundings to bfloat16 on the way count: a program that leaves them out, or rounds other values in their place, can miss the bound.
Values may be sent and summed in bfloat16 or wider, within the bound.
No kernel may reach another device: no remote copies, remote signals or barrier semaphores. Data moves between devices by JAX's collectives and lax.ppermute only.
A program may use at most 64 MiB of HBM per device.

v0:
```python
import math
import jax
import jax.numpy as jnp
from jax import lax
from jax.sharding import PartitionSpec as P

HEAD_SIZE = 128
SUMM = 50
adapter_scale = 2.0


def group_grads(query_group, key_group, value_group, cot_group, key_mask):
    softmax_scale = 1.0 / math.sqrt(HEAD_SIZE)
    scores = (
        jnp.einsum("tgd,md->gtm", query_group, key_group, preferred_element_type=jnp.float32)
        * softmax_scale
    )
    unnorm = jnp.exp(jnp.where(key_mask[None], scores, -jnp.inf))
    attend = unnorm / jnp.sum(unnorm, -1, keepdims=True)
    attend_grad = jnp.einsum(
        "tgd,md->gtm", cot_group, value_group, preferred_element_type=jnp.float32
    )
    row_dot = jnp.sum(attend * attend_grad, -1, keepdims=True)
    dscore = (attend * (attend_grad - row_dot)).astype(jnp.bfloat16)
    attend_low = attend.astype(jnp.bfloat16)
    query_grad = (
        jnp.einsum("gtm,md->tgd", dscore, key_group, preferred_element_type=jnp.float32)
        * softmax_scale
    )
    key_grad = (
        jnp.einsum("gtm,tgd->md", dscore, query_group, preferred_element_type=jnp.float32)
        * softmax_scale
    )
    value_grad = jnp.einsum(
        "gtm,tgd->md", attend_low, cot_group, preferred_element_type=jnp.float32
    )
    return (query_grad, key_grad, value_grad)


def adapter_terms(hidden_piece, low_rank_piece, value_piece, adapter_up_weight):
    contract = (((0,), (0,)), ((), ()))
    backward_step = lax.dot_general(
        value_piece, adapter_up_weight, (((1,), (1,)), ((), ())), preferred_element_type=jnp.float32
    ).astype(jnp.bfloat16)
    down_part = lax.dot_general(
        hidden_piece, backward_step, contract, preferred_element_type=jnp.float32
    )
    up_part = lax.dot_general(
        low_rank_piece, value_piece, contract, preferred_element_type=jnp.float32
    )
    return (down_part, up_part)


def per_device(
    queries,
    rotated_key_rows,
    values,
    cotangent,
    hidden,
    adapter_down_weight,
    adapter_up_weight,
    segment_text_length,
):
    query_rows = queries[0, 0]
    key_local = rotated_key_rows[0, 0]
    value_local = values[0, 0]
    cot_rows = cotangent[0, 0]
    hidden_row_block = hidden[0, 0]
    length = segment_text_length[0, 0]
    position = lax.axis_index("ctx")
    segment_list = lax.axis_size("ctx")
    log_batch = lax.axis_size("dp")
    tokens = query_rows.shape[0]
    width = key_local.shape[1]
    kv_heads = width // HEAD_SIZE
    groups = query_rows.shape[1] // width
    live = length + SUMM
    rows = jnp.arange(tokens)
    cot_rows = jnp.where((rows < live)[:, None], cot_rows, jnp.zeros_like(cot_rows))
    own_keys = lax.dynamic_slice_in_dim(key_local, length, SUMM, 0)
    own_values = lax.dynamic_slice_in_dim(value_local, length, SUMM, 0)
    memory_keys, memory_values = (
        lax.all_gather(own_keys, "ctx", axis=0, tiled=True),
        lax.all_gather(own_values, "ctx", axis=0, tiled=True),
    )
    count = memory_keys.shape[0]
    memory_owner = jnp.arange(count) // SUMM
    local_mask = (rows[None, :] <= rows[:, None]) & (rows[None, :] < live)
    memory_mask = jnp.broadcast_to((memory_owner < position)[None, :], (tokens, count))
    key_mask = jnp.concatenate([memory_mask, local_mask], axis=1)
    all_keys = jnp.concatenate([memory_keys, key_local], 0)
    all_values = jnp.concatenate([memory_values, value_local], 0)
    query_parts, key_parts, value_parts = ([], [], [])
    for group in range(kv_heads):
        qcols = slice(group * groups * HEAD_SIZE, (group + 1) * groups * HEAD_SIZE)
        kcols = slice(group * HEAD_SIZE, (group + 1) * HEAD_SIZE)
        query_grad, key_grad, value_grad = group_grads(
            query_rows[:, qcols].reshape(tokens, groups, HEAD_SIZE),
            all_keys[:, kcols],
            all_values[:, kcols],
            cot_rows[:, qcols].reshape(tokens, groups, HEAD_SIZE),
            key_mask,
        )
        query_parts.append(query_grad.reshape(tokens, groups * HEAD_SIZE))
        key_parts.append(key_grad)
        value_parts.append(value_grad)
    query_out = jnp.concatenate(query_parts, 1).astype(jnp.bfloat16)
    key_grad = jnp.concatenate(key_parts, 1)
    value_grad = jnp.concatenate(value_parts, 1)
    memory_key_grad, local_key = (key_grad[:count], key_grad[count:])
    memory_value_grad, local_value = (value_grad[:count], value_grad[count:])
    back_key, back_value = (
        lax.psum_scatter(memory_key_grad, "ctx", scatter_dimension=0, tiled=True),
        lax.psum_scatter(memory_value_grad, "ctx", scatter_dimension=0, tiled=True),
    )
    key_out = (
        local_key + lax.dynamic_update_slice_in_dim(jnp.zeros_like(local_key), back_key, length, 0)
    ).astype(jnp.bfloat16)
    value_result = (
        local_value
        + lax.dynamic_update_slice_in_dim(jnp.zeros_like(local_value), back_value, length, 0)
    ).astype(jnp.bfloat16)
    low_rank_rows = jnp.dot(
        hidden_row_block, adapter_down_weight, preferred_element_type=jnp.float32
    ).astype(jnp.bfloat16)
    down_sum, up_sum = lax.psum(
        adapter_terms(hidden_row_block, low_rank_rows, value_result, adapter_up_weight),
        ("dp", "ctx"),
    )
    adapter_factor = adapter_scale / (log_batch * segment_list)
    return (
        query_out[None, None],
        key_out[None, None],
        value_result[None, None],
        down_sum * adapter_factor,
        up_sum * adapter_factor,
    )


def solution(mesh):
    placed = (
        P("dp", "ctx", None, None),
        P("dp", "ctx", None, None),
        P("dp", "ctx", None, None),
        P("dp", "ctx", None, None),
        P("dp", "ctx", None, None),
        P(),
        P(),
        P("dp", "ctx"),
    )
    return jax.shard_map(
        per_device,
        mesh=mesh,
        in_specs=placed,
        out_specs=(
            P("dp", "ctx", None, None),
            P("dp", "ctx", None, None),
            P("dp", "ctx", None, None),
            P(),
            P(),
        ),
        check_vma=False,
    )
```

profile of v0, /device:TPU:23, one launch (start us, length us, event | category | flops | bytes accessed | tf_op | source)
XLA Modules:
  0.0 690.2 jit_solution(10573385685993678899)
XLA Ops:
  12.5 56.8 %all-gather.1 = bf16[1,1,800,512]{3,1,0,2:T(2,128)(2,1)S(1)} all-gather(bf16[1,1,50,512]{3,1,0,2:T(2,128)(2,1)S(1)} %copy.106), channel_id=3, replica_groups=mesh['dp'=32,'ctx'=16] {'ctx'}, dimensions={2}, use_global_device_ids=true | all-gather | bytes 870400 | tf_op jit(solution)/shard_map/all_gather | solution.py:84
  69.5 58.1 %all-gather = bf16[1,1,800,512]{3,1,0,2:T(2,128)(2,1)S(1)} all-gather(bf16[1,1,50,512]{3,1,0,2:T(2,128)(2,1)S(1)} %copy.105), channel_id=2, replica_groups=mesh['dp'=32,'ctx'=16] {'ctx'}, dimensions={2}, use_global_device_ids=true | all-gather | bytes 870400 | tf_op jit(solution)/shard_map/all_gather | solution.py:83
  134.7 3.7 fusion.6
  138.4 2.1 convolution_bitcast_fusion.2
  144.6 4.1 fusion.2
  148.7 2.9 convolution_bitcast_fusion.1
  151.6 1.8 fusion.4
  154.6 4.3 fusion.10
  158.9 2.9 convolution_bitcast_fusion.3
  161.8 1.8 fusion.12
  165.8 4.2 fusion.14
  170.0 2.1 convolution_bitcast_fusion.4
  172.2 2.0 fusion.16
  175.7 1.9 pad_maximum_fusion
  177.5 77.3 %fusion.89 = (f32[56,512]{1,0:T(8,128)}, f32[56,512]{1,0:T(8,128)}) fusion(f32[800,512]{1,0:T(8,128)} %get-tuple-element.26, f32[800,512]{1,0:T(8,128)} %get-tuple-element.25), kind=kCustom, calls=%all-reduce-scatter.2 | all-reduce-scatter fusion | flops 917505 | bytes 3508224
  254.8 2.0 collective-permute-start.2
  258.4 1.9 collective-permute-start.3
  260.3 1.9 collective-permute-start
  263.8 12.0 %collective-permute-start.1 = (f32[34,512]{1,0:T(8,128)}, f32[34,512]{1,0:T(8,128)}, u32[]{:S(2)}, u32[]{:S(2)}) collective-permute-start(f32[34,512]{1,0:T(8,128)} %slice.106), channel_id=1, source_target_pairs={{0,2},{1,3},{2,4},{3,5},{4,6},{5,7},{6,8},{7,9},{8,10},{9,11},{10,... | collective-permute-start | bytes 208904
  275.7 2.2 fusion.24
  289.3 2.8 concatenate.44
  293.7 2.8 concatenate.45
  298.6 116.7 %psum.15 = f32[16,512]{1,0:T(8,128)S(1)} all-reduce(f32[16,512]{1,0:T(8,128)S(1)} %fusion.26), channel_id=1, replica_groups=mesh['dp'=32,'ctx'=16] {'dp','ctx'}, use_global_device_ids=true, to_apply=%region_11.12 | all-reduce | flops 8192 | bytes 65536 | tf_op jit(solution)/shard_map/psum | solution.py:126
  417.1 264.6 %all-reduce.7.cloned.1.call-done = f32[4096,16]{0,1:T(8,128)} async-done(((f32[4096,16]{0,1:T(8,128)}), f32[4096,16]{0,1:T(8,128)}) %all-reduce.7.cloned.1.call-update) | async-done | bytes 262160 | tf_op jit(solution)/shard_map/psum | solution.py:126
  (139 shorter events, 41.2 us)
Async XLA Ops:
  7.2 290.9 %copy-start = (bf16[1,1,128,4096]{3,2,1,0:T(8,128)(2,1)S(1)}, bf16[1,1,128,4096]{3,2,1,0:T(8,128)(2,1)}, u32[]{:S(2)}) copy-start(bf16[1,1,128,4096]{3,2,1,0:T(8,128)(2,1)} %param.12) | copy-start | bytes 3145732
  7.2 4.9 copy-start.31
  7.2 674.5 %all-reduce.7.cloned.1.call-start = ((), (), s32[]{:S(2)}) async-start(), calls=%async_computation | async-start | bytes 524288 | tf_op jit(solution)/shard_map/psum | solution.py:126
  12.1 132.5 %copy-start.34 = (bf16[128,512]{0,1:T(8,128)(2,1)}, bf16[128,512]{0,1:T(8,128)(2,1)S(1)}, u32[]{:S(2)}) copy-start(bf16[128,512]{0,1:T(8,128)(2,1)S(1)} %get-tuple-element.14) | copy-start | bytes 393220
  12.5 117.0 %copy-start.26 = (bf16[128,512]{0,1:T(8,128)(2,1)}, bf16[128,512]{0,1:T(8,128)(2,1)S(1)}, u32[]{:S(2)}) copy-start(bf16[128,512]{0,1:T(8,128)(2,1)S(1)} %get-tuple-element.12) | copy-start | bytes 393220
  69.5 58.3 %copy-start.24 = (bf16[1,1,128,512]{3,2,1,0:T(8,128)(2,1)S(1)}, bf16[1,1,128,512]{3,2,1,0:T(8,128)(2,1)}, u32[]{:S(2)}) copy-start(bf16[1,1,128,512]{3,2,1,0:T(8,128)(2,1)} %param.10) | copy-start | bytes 393220
  134.7 9.9 %copy-start.37 = (pred[128,928]{0,1:T(8,128)(4,1)}, pred[128,928]{0,1:T(8,128)(4,1)S(1)}, u32[]{:S(2)}) copy-start(pred[128,928]{0,1:T(8,128)(4,1)S(1)} %pad_add_fusion) | copy-start | bytes 356356
  134.7 9.9 %copy-start.27 = (bf16[928,128,1]{1,0,2:T(8,128)(2,1)}, bf16[928,128,1]{1,0,2:T(8,128)(2,1)S(1)}, u32[]{:S(2)}) copy-start(bf16[928,128,1]{1,0,2:T(8,128)(2,1)S(1)} %fusion.64) | copy-start | bytes 712708
  172.1 3.5 copy-start.14
  172.1 3.5 copy-start.10
  172.1 3.5 copy-start.12
  172.2 3.5 copy-start.16
  172.2 3.5 copy-start.18
  254.8 23.1 %copy-start.28 = (bf16[928,128,1]{1,0,2:T(8,128)(2,1)S(1)}, bf16[928,128,1]{1,0,2:T(8,128)(2,1)}, u32[]{:S(2)}) copy-start(bf16[928,128,1]{1,0,2:T(8,128)(2,1)} %copy-done.27) | copy-start | bytes 712708
  254.8 24.1 %copy-start.3 = (bf16[4,128,928]{1,2,0:T(8,128)(2,1)S(1)}, bf16[4,128,928]{1,2,0:T(8,128)(2,1)}, u32[]{:S(2)}) copy-start(bf16[4,128,928]{1,2,0:T(8,128)(2,1)} %copy-done.2) | copy-start | bytes 2850820
  254.8 38.9 %collective-permute-start.2 = (f32[56,512]{1,0:T(8,128)}, f32[56,512]{1,0:T(8,128)}, u32[]{:S(2)}, u32[]{:S(2)}) collective-permute-start(f32[56,512]{1,0:T(8,128)} %get-tuple-element.8), channel_id=1, source_target_pairs={{0,1},{1,2},{2,3},{3,4},{4,5},{5,6},{6,7},{7,8},{8,9},{9,10},{10,1... | collective-permute-start | bytes 344072
  258.4 35.3 %collective-permute-start.3 = (f32[34,512]{1,0:T(8,128)}, f32[34,512]{1,0:T(8,128)}, u32[]{:S(2)}, u32[]{:S(2)}) collective-permute-start(f32[34,512]{1,0:T(8,128)} %slice.107), channel_id=1, source_target_pairs={{0,2},{1,3},{2,4},{3,5},{4,6},{5,7},{6,8},{7,9},{8,10},{9,11},{10,... | collective-permute-start | bytes 208904
  260.3 28.9 %collective-permute-start = (f32[56,512]{1,0:T(8,128)}, f32[56,512]{1,0:T(8,128)}, u32[]{:S(2)}, u32[]{:S(2)}) collective-permute-start(f32[56,512]{1,0:T(8,128)} %get-tuple-element.7), channel_id=1, source_target_pairs={{0,1},{1,2},{2,3},{3,4},{4,5},{5,6},{6,7},{7,8},{8,9},{9,10},{10,1... | collective-permute-start | bytes 344072
  263.8 25.5 %collective-permute-start.1 = (f32[34,512]{1,0:T(8,128)}, f32[34,512]{1,0:T(8,128)}, u32[]{:S(2)}, u32[]{:S(2)}) collective-permute-start(f32[34,512]{1,0:T(8,128)} %slice.106), channel_id=1, source_target_pairs={{0,2},{1,3},{2,4},{3,5},{4,6},{5,7},{6,8},{7,9},{8,10},{9,11},{10,... | collective-permute-start | bytes 208904
  281.0 8.2 %copy-start.11 = (f32[928,128]{1,0:T(8,128)S(1)}, f32[928,128]{1,0:T(8,128)}, u32[]{:S(2)}) copy-start(f32[928,128]{1,0:T(8,128)} %convolution_bitcast_fusion.1) | copy-start | bytes 1425412
  281.0 8.2 %copy-start.13 = (f32[928,128]{1,0:T(8,128)S(1)}, f32[928,128]{1,0:T(8,128)}, u32[]{:S(2)}) copy-start(f32[928,128]{1,0:T(8,128)} %convolution_bitcast_fusion.3) | copy-start | bytes 1425412
  281.0 8.2 %copy-start.15 = (f32[928,128]{1,0:T(8,128)S(1)}, f32[928,128]{1,0:T(8,128)}, u32[]{:S(2)}) copy-start(f32[928,128]{1,0:T(8,128)} %copy-done.14) | copy-start | bytes 1425412
  289.2 8.9 %copy-start.36 = (bf16[4096,16]{0,1:T(8,128)(2,1)S(1)}, bf16[4096,16]{0,1:T(8,128)(2,1)}, u32[]{:S(2)}) copy-start(bf16[4096,16]{0,1:T(8,128)(2,1)} %param.13) | copy-start | bytes 393220
  292.2 123.2 %copy-start.38 = (bf16[16,512]{1,0:T(8,128)(2,1)S(1)}, bf16[16,512]{1,0:T(8,128)(2,1)}, u32[]{:S(2)}) copy-start(bf16[16,512]{1,0:T(8,128)(2,1)} %param.14) | copy-start | bytes 49156
  (23 other events, 48.4 us)
Sparse Core Ops, SparseCore 0:
  416.6 265.0 all-reduce.6
where the time goes:
time: 691 us; the launch traced here: 690 us
  blocking collectives  309 us (45%)
  waiting for transfers between devices  265 us (38%)
  matrix products  43.7 us (6%)
  local copies, waits for them, and re-layouts  23.8 us (3%)
  starting transfers between devices  17.9 us (3%)
  between operations  16 us (2%)
  other arithmetic  15.3 us (2%)
    psum x1, waiting for transfers between devices, per_device(): lax.psum(adapter_terms(hidden_row_block, low_rank_rows, value_result, ada...  265 us
    psum x1, blocking collectives, per_device(): lax.psum(adapter_terms(hidden_row_block, low_rank_rows, value_result, ada...  117 us
    unnamed x1, blocking collectives  77.3 us
    all_gather x1, blocking collectives, per_device(): lax.all_gather(own_keys, 'ctx', axis=0, tiled=True)  58.1 us
    all_gather x1, blocking collectives, per_device(): lax.all_gather(own_values, 'ctx', axis=0, tiled=True)  56.8 us
    unnamed x4, starting transfers between devices  17.8 us
    div x4, matrix products, group_grads(): attend = unnorm / jnp.sum(unnorm, -1, keepdims=True)  16.4 us
    unnamed x95, local copies, waits for them, and re-layouts  16.1 us
  transfers between devices with their start and end apart: 5, of which 1 were waited for; matrix products, arithmetic and copies ran while one was open for 3% of the time, Pallas kernels for 0%

commit v1 on v0

--- a/solution.py
+++ b/solution.py
@@ -79,8 +79,15 @@
     cot_rows = jnp.where((rows < live)[:, None], cot_rows, jnp.zeros_like(cot_rows))
     own_keys = lax.dynamic_slice_in_dim(key_local, length, SUMM, 0)
     own_values = lax.dynamic_slice_in_dim(value_local, length, SUMM, 0)
+
+    def create_scales_on(array_in):
+        return jnp.concatenate(
+            lax.all_to_all(jnp.stack([array_in for _ in range(lax.axis_size("ctx"))]), "ctx", 0, 0),
+            axis=0,
+        )
+
     memory_keys, memory_values = (
-        lax.all_gather(own_keys, "ctx", axis=0, tiled=True),
+        create_scales_on(own_keys),
         lax.all_gather(own_values, "ctx", axis=0, tiled=True),
     )
     count = memory_keys.shape[0]

time: 691 us -> 653 us (0.945)
  blocking collectives: 309 us -> 243 us
  starting transfers between devices: 17.9 us -> 51.1 us
    all_gather x1 -> x0, blocking collectives: 58.1 us -> none  [per_device(): lax.all_gather(own_keys, 'ctx', axis=0, tiled=True)]
    unnamed x4, starting transfers between devices: 17.8 us -> 35.8 us
    all_to_all x0 -> x1, starting transfers between devices: none -> 15.3 us  [create_scales_on(): lax.all_to_all(jnp.stack([array_in for _ in range(lax.axis_size('ctx'))])...]
    psum x1, blocking collectives: 117 us -> 103 us  [per_device(): lax.psum(adapter_terms(hidden_row_block, low_rank_rows, value_result, ada...]
    all_gather x1, blocking collectives: 56.8 us -> 67.9 us  [per_device(): lax.all_gather(own_values, 'ctx', axis=0, tiled=True)]
    unnamed x95 -> x83, local copies, waits for them, and re-layouts: 16.1 us -> 11.7 us
  transfers between devices with their start and end apart: 5 -> 6, of which waited for: 1 -> 2; matrix products, arithmetic and copies ran while one was open for 3% -> 3% of each run, Pallas kernels for 0% -> 0%
where the time goes in v1:
time: 653 us; the launch traced here: 652 us
  waiting for transfers between devices  264 us (40%)
  blocking collectives  243 us (37%)
  starting transfers between devices  51.1 us (8%)
  matrix products  40 us (6%)
  local copies, waits for them, and re-layouts  20.4 us (3%)
  other arithmetic  16.2 us (2%)
  between operations  16 us (2%)
    psum x1, waiting for transfers between devices, per_device(): lax.psum(adapter_terms(hidden_row_block, low_rank_rows, value_result, ada...  263 us
    psum x1, blocking collectives, per_device(): lax.psum(adapter_terms(hidden_row_block, low_rank_rows, value_result, ada...  103 us
    unnamed x1, blocking collectives  72.3 us
    all_gather x1, blocking collectives, per_device(): lax.all_gather(own_values, 'ctx', axis=0, tiled=True)  67.9 us
    unnamed x4, starting transfers between devices  35.8 us
    all_to_all x1, starting transfers between devices, create_scales_on(): lax.all_to_all(jnp.stack([array_in for _ in range(lax.axis_size('ctx'))])...  15.3 us
    div x4, matrix products, group_grads(): attend = unnorm / jnp.sum(unnorm, -1, keepdims=True)  14.7 us
  transfers between devices with their start and end apart: 6, of which 2 were waited for; matrix products, arithmetic and copies ran while one was open for 3% of the time, Pallas kernels for 0%

profile of v1, /device:TPU:23, one launch (start us, length us, event | category | flops | bytes accessed | tf_op | source)
XLA Modules:
  0.0 651.7 jit_solution(14758997393797035077)
XLA Ops:
  9.9 15.3 %all-to-all-start = ((bf16[16,50,512]{2,1,0:T(8,128)(2,1)}), bf16[16,50,512]{2,1,0:T(8,128)(2,1)S(1)}, u32[]{:S(2)}, u32[]{:S(2)}) async-start(bf16[16,50,512]{2,1,0:T(8,128)(2,1)} %stack.5), calls=%async_computation | async-start | bytes 1835008 | tf_op jit(solution)/shard_map/all_to_all | solution.py:85
  28.0 67.9 %all-gather = bf16[1,1,800,512]{3,1,0,2:T(2,128)(2,1)S(1)} all-gather(bf16[1,1,50,512]{3,1,0,2:T(2,128)(2,1)S(1)} %copy.102), channel_id=2, replica_groups=mesh['dp'=32,'ctx'=16] {'ctx'}, dimensions={2}, use_global_device_ids=true | all-gather | bytes 870400 | tf_op jit(solution)/shard_map/all_gather | solution.py:91
  106.6 3.7 fusion.6
  110.3 2.1 convolution_bitcast_fusion.2
  112.4 1.8 fusion.8
  115.6 3.8 fusion.2
  119.4 2.9 convolution_bitcast_fusion.1
  122.3 1.8 fusion.4
  126.3 3.7 fusion.10
  130.0 2.9 convolution_bitcast_fusion.3
  132.9 1.8 fusion.12
  136.9 3.6 fusion.14
  140.5 2.1 convolution_bitcast_fusion.4
  142.6 2.0 fusion.16
  146.8 2.4 pad_maximum_fusion
  149.2 72.3 %fusion.89 = (f32[56,512]{1,0:T(8,128)}, f32[56,512]{1,0:T(8,128)S(1)}) fusion(f32[800,512]{1,0:T(8,128)} %get-tuple-element.26, f32[800,512]{1,0:T(8,128)S(1)} %get-tuple-element.25), kind=kCustom, calls=%all-reduce-scatter.2 | all-reduce-scatter fusion | flops 917505 | bytes 3508224
  223.1 2.1 collective-permute-start
  225.8 1.9 collective-permute-start.2
  231.9 12.6 %collective-permute-start.3 = (f32[34,512]{1,0:T(8,128)}, f32[34,512]{1,0:T(8,128)}, u32[]{:S(2)}, u32[]{:S(2)}) collective-permute-start(f32[34,512]{1,0:T(8,128)} %slice.107), channel_id=1, source_target_pairs={{0,2},{1,3},{2,4},{3,5},{4,6},{5,7},{6,8},{7,9},{8,10},{9,11},{10,... | collective-permute-start | bytes 208904
  244.5 19.1 %collective-permute-start.1 = (f32[34,512]{1,0:T(8,128)}, f32[34,512]{1,0:T(8,128)S(1)}, u32[]{:S(2)}, u32[]{:S(2)}) collective-permute-start(f32[34,512]{1,0:T(8,128)} %slice.106), channel_id=1, source_target_pairs={{0,2},{1,3},{2,4},{3,5},{4,6},{5,7},{6,8},{7,9},{8,10},{9,11},{10,... | collective-permute-start | bytes 208904
  266.9 2.0 concatenate.44
  270.5 2.0 concatenate.45
  274.6 103.3 %psum.15 = f32[16,512]{1,0:T(8,128)S(1)} all-reduce(f32[16,512]{1,0:T(8,128)S(1)} %fusion.26), channel_id=1, replica_groups=mesh['dp'=32,'ctx'=16] {'dp','ctx'}, use_global_device_ids=true, to_apply=%region_11.12 | all-reduce | flops 8192 | bytes 65536 | tf_op jit(solution)/shard_map/psum | solution.py:133
  379.7 263.5 %all-reduce.7.cloned.1.call-done = f32[4096,16]{0,1:T(8,128)} async-done(((f32[4096,16]{0,1:T(8,128)}), f32[4096,16]{0,1:T(8,128)}) %all-reduce.7.cloned.1.call-update) | async-done | bytes 262160 | tf_op jit(solution)/shard_map/psum | solution.py:133
  (130 shorter events, 39.2 us)
Async XLA Ops:
  7.2 266.9 %copy-start = (bf16[1,1,128,4096]{3,2,1,0:T(8,128)(2,1)S(1)}, bf16[1,1,128,4096]{3,2,1,0:T(8,128)(2,1)}, u32[]{:S(2)}) copy-start(bf16[1,1,128,4096]{3,2,1,0:T(8,128)(2,1)} %param.12) | copy-start | bytes 3145732
  7.2 18.3 %copy-start.13 = (bf16[1,1,128,512]{3,2,1,0:T(8,128)(2,1)S(1)}, bf16[1,1,128,512]{3,2,1,0:T(8,128)(2,1)}, u32[]{:S(2)}) copy-start(bf16[1,1,128,512]{3,2,1,0:T(8,128)(2,1)} %param.10) | copy-start | bytes 393220
  7.2 18.4 %copy-start.24 = (bf16[1,1,128,2048]{3,2,1,0:T(8,128)(2,1)S(1)}, bf16[1,1,128,2048]{3,2,1,0:T(8,128)(2,1)}, u32[]{:S(2)}) copy-start(bf16[1,1,128,2048]{3,2,1,0:T(8,128)(2,1)} %param.8) | copy-start | bytes 1572868
  9.9 95.7 %all-to-all-start = ((bf16[16,50,512]{2,1,0:T(8,128)(2,1)}), bf16[16,50,512]{2,1,0:T(8,128)(2,1)S(1)}, u32[]{:S(2)}, u32[]{:S(2)}) async-start(bf16[16,50,512]{2,1,0:T(8,128)(2,1)} %stack.5), calls=%async_computation | async-start | bytes 1835008 | tf_op jit(solution)/shard_map/all_to_all | solution.py:85
  25.3 617.9 %all-reduce.7.cloned.1.call-start = ((), (), s32[]{:S(2)}) async-start(), calls=%async_computation.1 | async-start | bytes 524288 | tf_op jit(solution)/shard_map/psum | solution.py:133
  99.0 3.3 copy-start.15
  99.0 3.3 copy-start.17
  99.0 3.3 copy-start.19
  99.0 5.0 copy-start.21
  106.6 3.7 copy-start.22
  115.6 30.4 %copy-start.10 = (f32[928,128]{1,0:T(8,128)}, f32[928,128]{1,0:T(8,128)S(1)}, u32[]{:S(2)}) copy-start(f32[928,128]{1,0:T(8,128)S(1)} %fusion.19) | copy-start | bytes 1425412
  115.6 3.8 copy-start.20
  126.3 3.7 copy-start.18
  136.9 3.6 copy-start.16
  142.6 3.5 copy-start.9
  221.5 43.0 %copy-start.6 = (f32[928,128]{1,0:T(8,128)S(1)}, f32[928,128]{1,0:T(8,128)}, u32[]{:S(2)}) copy-start(f32[928,128]{1,0:T(8,128)} %convolution_bitcast_fusion.1) | copy-start | bytes 1425412
  221.5 43.0 %copy-start.8 = (f32[928,128]{1,0:T(8,128)S(1)}, f32[928,128]{1,0:T(8,128)}, u32[]{:S(2)}) copy-start(f32[928,128]{1,0:T(8,128)} %convolution_bitcast_fusion.3) | copy-start | bytes 1425412
  223.1 43.8 %collective-permute-start = (f32[56,512]{1,0:T(8,128)}, f32[56,512]{1,0:T(8,128)}, u32[]{:S(2)}, u32[]{:S(2)}) collective-permute-start(f32[56,512]{1,0:T(8,128)} %get-tuple-element.7), channel_id=1, source_target_pairs={{0,1},{1,2},{2,3},{3,4},{4,5},{5,6},{6,7},{7,8},{8,9},{9,10},{10,1... | collective-permute-start | bytes 344072
  225.8 44.6 %collective-permute-start.2 = (f32[56,512]{1,0:T(8,128)S(1)}, f32[56,512]{1,0:T(8,128)}, u32[]{:S(2)}, u32[]{:S(2)}) collective-permute-start(f32[56,512]{1,0:T(8,128)S(1)} %get-tuple-element.8), channel_id=1, source_target_pairs={{0,1},{1,2},{2,3},{3,4},{4,5},{5,6},{6,7},{7,8},{8,9},{9,10},{10,1... | collective-permute-start | bytes 344072
  229.8 37.1 %copy-start.23 = (f32[56,512]{1,0:T(8,128)S(1)}, f32[56,512]{1,0:T(8,128)}, u32[]{:S(2)}) copy-start(f32[56,512]{1,0:T(8,128)} %get-tuple-element.7) | copy-start | bytes 344068
  231.9 38.6 %collective-permute-start.3 = (f32[34,512]{1,0:T(8,128)}, f32[34,512]{1,0:T(8,128)}, u32[]{:S(2)}, u32[]{:S(2)}) collective-permute-start(f32[34,512]{1,0:T(8,128)} %slice.107), channel_id=1, source_target_pairs={{0,2},{1,3},{2,4},{3,5},{4,6},{5,7},{6,8},{7,9},{8,10},{9,11},{10,... | collective-permute-start | bytes 208904
  244.5 21.7 %collective-permute-start.1 = (f32[34,512]{1,0:T(8,128)}, f32[34,512]{1,0:T(8,128)S(1)}, u32[]{:S(2)}, u32[]{:S(2)}) collective-permute-start(f32[34,512]{1,0:T(8,128)} %slice.106), channel_id=1, source_target_pairs={{0,2},{1,3},{2,4},{3,5},{4,6},{5,7},{6,8},{7,9},{8,10},{9,11},{10,... | collective-permute-start | bytes 208904
  265.4 8.7 %copy-start.32 = (bf16[4096,16]{0,1:T(8,128)(2,1)S(1)}, bf16[4096,16]{0,1:T(8,128)(2,1)}, u32[]{:S(2)}) copy-start(bf16[4096,16]{0,1:T(8,128)(2,1)} %param.13) | copy-start | bytes 393220
  268.9 108.9 %copy-start.36 = (bf16[16,512]{1,0:T(8,128)(2,1)S(1)}, bf16[16,512]{1,0:T(8,128)(2,1)}, u32[]{:S(2)}) copy-start(bf16[16,512]{1,0:T(8,128)(2,1)} %param.14) | copy-start | bytes 49156
  (19 other events, 32.4 us)
Sparse Core Ops, SparseCore 0:
  379.2 263.9 all-reduce.6
